TPU v7x, 256 devices: a whole 4x4x8 slice. The times are simulated.
256 devices in a mesh: blk: 64 (over y, x_lo, z), team: 4 (over x_hi, core).
Axes of the slice: x: 4 (x_hi: 2, x_lo: 2; x = x_hi * 2 + x_lo), y: 4, z: 8, core: 2. Of those that a mesh axis runs over, the one named last changes fastest.
Arguments:
- loadings: bfloat16 [64, 98304], P(None, ('blk', 'team')), may hold values from -6 to 6
- scales: bfloat16 [64, 768], P(None, ('blk', 'team')), may hold values from 0.25 to 4
- cov: bfloat16 [16384, 16, 4, 1536], P('blk', None, 'team'), may hold values from -0.01953125 to 0.01953125
Outputs:
- product: float32 [64, 16384], P(None, 'blk')
All inputs are finite; a program needn't handle non-finite values.
Results may differ from a plain program's by a relative error of at most 0.0028.
Values may be sent and summed in bfloat16 or wider, within the bound.
No kernel may reach another device: no remote copies, remote signals or barrier semaphores. Data moves between devices by JAX's collectives and lax.ppermute only.
A program may use at most 128 MiB of HBM per device.

v0:
```python
import jax
import jax.numpy as jnp
from jax import lax
from jax.sharding import PartitionSpec as P


def passed_along(x, axis, by):
    size = lax.axis_size(axis)
    return lax.ppermute(x, axis, [(i, (i + by) % size) for i in range(size)])


def per_device(loadings, scales, cov):
    team_size = lax.axis_size("team")
    cycle_size = lax.axis_size("blk")
    cycle_stops = cycle_size // team_size
    cycle_pos = lax.axis_index("blk")
    member = lax.axis_index("team")
    skew_lag = jnp.mod(cycle_pos - member, team_size)
    base_stop = jnp.mod((cycle_pos - skew_lag - member) // team_size, cycle_stops)
    held_block = (
        lax.all_gather(loadings, "team", axis=1, tiled=True),
        lax.all_gather(scales, "team", axis=1, tiled=True),
    )
    near_copy = passed_along((held_block[0], held_block[1]), "blk", 1)
    far_copies = passed_along((held_block[0], held_block[1], near_copy[0], near_copy[1]), "blk", 2)
    stacked_loads = jnp.stack([held_block[0], near_copy[0], far_copies[0], far_copies[2]])
    stacked_scales = jnp.stack([held_block[1], near_copy[1], far_copies[1], far_copies[3]])
    start_block = (
        lax.dynamic_index_in_dim(stacked_loads, skew_lag, 0, keepdims=False),
        lax.dynamic_index_in_dim(stacked_scales, skew_lag, 0, keepdims=False),
    )
    cov_local = cov[:, :, 0, :]
    n_loads = loadings.shape[0]
    row_count = cov.shape[0]

    def contribute(running, block, stop_num):
        block_load, block_scale = block
        groups = block_scale.shape[1]
        scaled = (
            (
                block_load.astype(jnp.float32).reshape(
                    n_loads, groups, block_load.shape[1] // groups
                )
                * block_scale.astype(jnp.float32)[:, :, None]
            )
            .reshape(n_loads, block_load.shape[1])
            .astype(jnp.bfloat16)
        )
        cov_slab = lax.dynamic_index_in_dim(
            cov_local, jnp.mod(stop_num, cycle_stops), 1, keepdims=False
        )
        term = lax.dot_general(
            scaled, cov_slab, (((1,), (1,)), ((), ())), preferred_element_type=jnp.float32
        )
        return running + term

    initial = jnp.zeros((n_loads, row_count), jnp.float32)
    running = contribute(initial, start_block, base_stop)

    def onward(stop_num, carry):
        partial_sum, moving = carry
        moving = passed_along((moving[0], moving[1]), "blk", team_size)
        return (contribute(partial_sum, moving, base_stop - stop_num), moving)

    running, _ = lax.fori_loop(1, cycle_stops, onward, (running, start_block))
    product = lax.psum(running, "team")
    return product


def solution(mesh):
    placed = (P(None, ("blk", "team")), P(None, ("blk", "team")), P("blk", None, "team", None))
    return jax.shard_map(
        per_device, mesh=mesh, in_specs=placed, out_specs=P(None, "blk"), check_vma=False
    )
```

profile of v0, /device:TPU:1, one launch (start us, length us, event | category | flops | bytes accessed | tf_op | source)
XLA Modules:
  0.0 371.3 jit_solution(5446585981449639470)
XLA Ops:
  6.5 10.4 %all_gather.6 = bf16[64,1536]{1,0:T(8,128)(2,1)S(1)} all-gather(bf16[64,384]{1,0:T(8,128)(2,1)} %param.5), channel_id=1, replica_groups=mesh['blk'=64,'team'=4] {'team'}, dimensions={1}, use_global_device_ids=true | all-gather | bytes 245760 | tf_op jit(solution)/shard_map/all_gather | solution.py:21
  16.9 2.9 collective-permute-start.3
  19.8 7.4 %all-gather = bf16[4,3,64]{2,1,0:T(4,128)(2,1)S(1)} all-gather(bf16[1,3,64]{2,1,0:T(4,128)(2,1)} %bitcast.55), channel_id=1, replica_groups=mesh['blk'=64,'team'=4] {'team'}, dimensions={0}, use_global_device_ids=true | all-gather | bytes 1920 | tf_op jit(solution)/shard_map/all_gather | solution.py:22
  27.2 2.9 collective-permute-start.5
  30.0 1.2 collective-permute-start.6
  31.2 6.3 %collective-permute-done.5 = bf16[64,12]{0,1:T(8,128)(2,1)S(1)} collective-permute-done((bf16[64,12]{0,1:T(8,128)(2,1)S(1)}, bf16[64,12]{0,1:T(8,128)(2,1)S(1)}, u32[]{:S(2)}, u32[]{:S(2)}) %collective-permute-start.5) | collective-permute-done | bytes 1568 | tf_op jit(solution)/shard_map/ppermute | solution.py:9
  37.6 0.7 collective-permute-start.4
  38.2 4.4 %constant_dynamic-slice_fusion = bf16[256,1,1,1536]{3,1,2,0:T(2,128)(2,1)S(1)} fusion(bf16[256,16,1,1536]{3,1,2,0:T(8,128)(2,1)} %param.7, s32[]{:T(128)S(6)} %select_n.61), kind=kLoop, calls=%fused_computation.27 | loop fusion | bytes 1572868 | tf_op jit(solution)/shard_map/jit(dynamic_index_in_dim)/dynamic_slice | solution.py:49
  42.7 13.0 %copy.27 = bf16[256,16,1,1536]{3,0,1,2:T(8,128)(2,1)} copy(bf16[256,16,1,1536]{3,1,2,0:T(8,128)(2,1)} %param.7) | data formatting | bytes 25165824 | tf_op args[2]
  56.3 0.2 multiply_convert_fusion
  56.5 0.4 fusion.5
  56.8 219.6 %while.19 = (s32[]{:T(128)}, f32[64,256]{1,0:T(8,128)S(1)}, bf16[64,1536]{1,0:T(8,128)(2,1)S(1)}, bf16[64,12]{1,0:T(8,128)(2,1)S(1)}, s32[]{:T(128)}, /*index=5*...) while((s32[]{:T(128)}, f32[64,256]{1,0:T(8,128)S(1)}, ...), condition=%wide.region_1.2_spmd, body=%wide.region_0.1_spmd.sunk | while | flops 50642960 | bytes 3091284 | solution.py:65
  56.9 2.6 collective-permute-start.1
  59.4 3.8 %collective-permute-start = (bf16[64,12]{1,0:T(8,128)(2,1)S(1)}, bf16[64,12]{1,0:T(8,128)(2,1)S(1)}, u32[]{:S(2)}, u32[]{:S(2)}) collective-permute-start(bf16[64,12]{1,0:T(8,128)(2,1)S(1)} %get-tuple-element.235), channel_id=1, source_target_pairs={{0,16},{4,20},{8,24},{12,28},{16,32},{20,36},{24,40},{28,44},{32,4... | collective-permute-start | bytes 4616 | tf_op jit(solution)/shard_map/while/body/eval_jaxpr/ppermute | solution.py:9
  63.2 8.5 %collective-permute-done = bf16[64,12]{1,0:T(8,128)(2,1)S(1)} collective-permute-done((bf16[64,12]{1,0:T(8,128)(2,1)S(1)}, bf16[64,12]{1,0:T(8,128)(2,1)S(1)}, u32[]{:S(2)}, u32[]{:S(2)}) %collective-permute-start) | collective-permute-done | bytes 1568 | tf_op jit(solution)/shard_map/while/body/eval_jaxpr/ppermute | solution.py:9
  71.7 0.2 mul.51
  71.9 1.5 convolution_add_fusion.2
  73.4 0.7 collective-permute-start.1
  74.2 5.7 %collective-permute-start = (bf16[64,12]{1,0:T(8,128)(2,1)S(1)}, bf16[64,12]{1,0:T(8,128)(2,1)S(1)}, u32[]{:S(2)}, u32[]{:S(2)}) collective-permute-start(bf16[64,12]{1,0:T(8,128)(2,1)S(1)} %get-tuple-element.235), channel_id=1, source_target_pairs={{0,16},{4,20},{8,24},{12,28},{16,32},{20,36},{24,40},{28,44},{32,4... | collective-permute-start | bytes 4616 | tf_op jit(solution)/shard_map/while/body/eval_jaxpr/ppermute | solution.py:9
  79.9 11.1 %collective-permute-done = bf16[64,12]{1,0:T(8,128)(2,1)S(1)} collective-permute-done((bf16[64,12]{1,0:T(8,128)(2,1)S(1)}, bf16[64,12]{1,0:T(8,128)(2,1)S(1)}, u32[]{:S(2)}, u32[]{:S(2)}) %collective-permute-start) | collective-permute-done | bytes 1568 | tf_op jit(solution)/shard_map/while/body/eval_jaxpr/ppermute | solution.py:9
  91.0 0.2 mul.51
  91.2 1.5 convolution_add_fusion.2
  92.8 2.0 collective-permute-start
  94.8 10.4 %collective-permute-done = bf16[64,12]{1,0:T(8,128)(2,1)S(1)} collective-permute-done((bf16[64,12]{1,0:T(8,128)(2,1)S(1)}, bf16[64,12]{1,0:T(8,128)(2,1)S(1)}, u32[]{:S(2)}, u32[]{:S(2)}) %collective-permute-start) | collective-permute-done | bytes 1568 | tf_op jit(solution)/shard_map/while/body/eval_jaxpr/ppermute | solution.py:9
  105.5 1.5 convolution_add_fusion.2
  107.0 3.6 collective-permute-start
  110.6 8.2 %collective-permute-done = bf16[64,12]{1,0:T(8,128)(2,1)S(1)} collective-permute-done((bf16[64,12]{1,0:T(8,128)(2,1)S(1)}, bf16[64,12]{1,0:T(8,128)(2,1)S(1)}, u32[]{:S(2)}, u32[]{:S(2)}) %collective-permute-start) | collective-permute-done | bytes 1568 | tf_op jit(solution)/shard_map/while/body/eval_jaxpr/ppermute | solution.py:9
  119.0 1.5 convolution_add_fusion.2
  120.6 4.6 %collective-permute-start = (bf16[64,12]{1,0:T(8,128)(2,1)S(1)}, bf16[64,12]{1,0:T(8,128)(2,1)S(1)}, u32[]{:S(2)}, u32[]{:S(2)}) collective-permute-start(bf16[64,12]{1,0:T(8,128)(2,1)S(1)} %get-tuple-element.235), channel_id=1, source_target_pairs={{0,16},{4,20},{8,24},{12,28},{16,32},{20,36},{24,40},{28,44},{32,4... | collective-permute-start | bytes 4616 | tf_op jit(solution)/shard_map/while/body/eval_jaxpr/ppermute | solution.py:9
  125.2 7.1 %collective-permute-done = bf16[64,12]{1,0:T(8,128)(2,1)S(1)} collective-permute-done((bf16[64,12]{1,0:T(8,128)(2,1)S(1)}, bf16[64,12]{1,0:T(8,128)(2,1)S(1)}, u32[]{:S(2)}, u32[]{:S(2)}) %collective-permute-start) | collective-permute-done | bytes 1568 | tf_op jit(solution)/shard_map/while/body/eval_jaxpr/ppermute | solution.py:9
  132.5 1.5 convolution_add_fusion.2
  134.1 5.4 %collective-permute-start = (bf16[64,12]{1,0:T(8,128)(2,1)S(1)}, bf16[64,12]{1,0:T(8,128)(2,1)S(1)}, u32[]{:S(2)}, u32[]{:S(2)}) collective-permute-start(bf16[64,12]{1,0:T(8,128)(2,1)S(1)} %get-tuple-element.235), channel_id=1, source_target_pairs={{0,16},{4,20},{8,24},{12,28},{16,32},{20,36},{24,40},{28,44},{32,4... | collective-permute-start | bytes 4616 | tf_op jit(solution)/shard_map/while/body/eval_jaxpr/ppermute | solution.py:9
  139.5 6.3 %collective-permute-done = bf16[64,12]{1,0:T(8,128)(2,1)S(1)} collective-permute-done((bf16[64,12]{1,0:T(8,128)(2,1)S(1)}, bf16[64,12]{1,0:T(8,128)(2,1)S(1)}, u32[]{:S(2)}, u32[]{:S(2)}) %collective-permute-start) | collective-permute-done | bytes 1568 | tf_op jit(solution)/shard_map/while/body/eval_jaxpr/ppermute | solution.py:9
  146.0 1.5 convolution_add_fusion.2
  147.5 0.3 collective-permute-start.1
  147.8 6.4 %collective-permute-start = (bf16[64,12]{1,0:T(8,128)(2,1)S(1)}, bf16[64,12]{1,0:T(8,128)(2,1)S(1)}, u32[]{:S(2)}, u32[]{:S(2)}) collective-permute-start(bf16[64,12]{1,0:T(8,128)(2,1)S(1)} %get-tuple-element.235), channel_id=1, source_target_pairs={{0,16},{4,20},{8,24},{12,28},{16,32},{20,36},{24,40},{28,44},{32,4... | collective-permute-start | bytes 4616 | tf_op jit(solution)/shard_map/while/body/eval_jaxpr/ppermute | solution.py:9
  154.2 5.0 %collective-permute-done = bf16[64,12]{1,0:T(8,128)(2,1)S(1)} collective-permute-done((bf16[64,12]{1,0:T(8,128)(2,1)S(1)}, bf16[64,12]{1,0:T(8,128)(2,1)S(1)}, u32[]{:S(2)}, u32[]{:S(2)}) %collective-permute-start) | collective-permute-done | bytes 1568 | tf_op jit(solution)/shard_map/while/body/eval_jaxpr/ppermute | solution.py:9
  159.4 1.5 convolution_add_fusion.2
  160.9 1.7 collective-permute-start.1
  162.6 3.0 collective-permute-start
  165.6 7.0 %collective-permute-done = bf16[64,12]{1,0:T(8,128)(2,1)S(1)} collective-permute-done((bf16[64,12]{1,0:T(8,128)(2,1)S(1)}, bf16[64,12]{1,0:T(8,128)(2,1)S(1)}, u32[]{:S(2)}, u32[]{:S(2)}) %collective-permute-start) | collective-permute-done | bytes 1568 | tf_op jit(solution)/shard_map/while/body/eval_jaxpr/ppermute | solution.py:9
  172.8 1.5 convolution_add_fusion.2
  174.3 0.8 collective-permute-start.1
  175.1 1.9 collective-permute-start
  177.0 10.0 %collective-permute-done = bf16[64,12]{1,0:T(8,128)(2,1)S(1)} collective-permute-done((bf16[64,12]{1,0:T(8,128)(2,1)S(1)}, bf16[64,12]{1,0:T(8,128)(2,1)S(1)}, u32[]{:S(2)}, u32[]{:S(2)}) %collective-permute-start) | collective-permute-done | bytes 1568 | tf_op jit(solution)/shard_map/while/body/eval_jaxpr/ppermute | solution.py:9
  187.1 1.5 convolution_add_fusion.2
  188.7 1.4 collective-permute-start
  190.2 12.2 %collective-permute-done = bf16[64,12]{1,0:T(8,128)(2,1)S(1)} collective-permute-done((bf16[64,12]{1,0:T(8,128)(2,1)S(1)}, bf16[64,12]{1,0:T(8,128)(2,1)S(1)}, u32[]{:S(2)}, u32[]{:S(2)}) %collective-permute-start) | collective-permute-done | bytes 1568 | tf_op jit(solution)/shard_map/while/body/eval_jaxpr/ppermute | solution.py:9
  202.6 1.5 convolution_add_fusion.2
  204.3 13.2 %collective-permute-done = bf16[64,12]{1,0:T(8,128)(2,1)S(1)} collective-permute-done((bf16[64,12]{1,0:T(8,128)(2,1)S(1)}, bf16[64,12]{1,0:T(8,128)(2,1)S(1)}, u32[]{:S(2)}, u32[]{:S(2)}) %collective-permute-start) | collective-permute-done | bytes 1568 | tf_op jit(solution)/shard_map/while/body/eval_jaxpr/ppermute | solution.py:9
  217.7 1.5 convolution_add_fusion.2
  219.4 14.1 %collective-permute-done = bf16[64,12]{1,0:T(8,128)(2,1)S(1)} collective-permute-done((bf16[64,12]{1,0:T(8,128)(2,1)S(1)}, bf16[64,12]{1,0:T(8,128)(2,1)S(1)}, u32[]{:S(2)}, u32[]{:S(2)}) %collective-permute-start) | collective-permute-done | bytes 1568 | tf_op jit(solution)/shard_map/while/body/eval_jaxpr/ppermute | solution.py:9
  233.8 1.5 convolution_add_fusion.2
  235.5 12.3 %collective-permute-done = bf16[64,12]{1,0:T(8,128)(2,1)S(1)} collective-permute-done((bf16[64,12]{1,0:T(8,128)(2,1)S(1)}, bf16[64,12]{1,0:T(8,128)(2,1)S(1)}, u32[]{:S(2)}, u32[]{:S(2)}) %collective-permute-start) | collective-permute-done | bytes 1568 | tf_op jit(solution)/shard_map/while/body/eval_jaxpr/ppermute | solution.py:9
  248.0 1.5 convolution_add_fusion.2
  249.6 0.5 collective-permute-start
  250.1 11.1 %collective-permute-done = bf16[64,12]{1,0:T(8,128)(2,1)S(1)} collective-permute-done((bf16[64,12]{1,0:T(8,128)(2,1)S(1)}, bf16[64,12]{1,0:T(8,128)(2,1)S(1)}, u32[]{:S(2)}, u32[]{:S(2)}) %collective-permute-start) | collective-permute-done | bytes 1568 | tf_op jit(solution)/shard_map/while/body/eval_jaxpr/ppermute | solution.py:9
  261.5 1.5 convolution_add_fusion.2
  263.0 1.1 collective-permute-start
  264.2 10.6 %collective-permute-done = bf16[64,12]{1,0:T(8,128)(2,1)S(1)} collective-permute-done((bf16[64,12]{1,0:T(8,128)(2,1)S(1)}, bf16[64,12]{1,0:T(8,128)(2,1)S(1)}, u32[]{:S(2)}, u32[]{:S(2)}) %collective-permute-start) | collective-permute-done | bytes 1568 | tf_op jit(solution)/shard_map/while/body/eval_jaxpr/ppermute | solution.py:9
  275.0 1.5 convolution_add_fusion.2
  276.5 0.6 copy-done
  277.1 85.8 %all-reduce.2.cloned.1.call-done = f32[64,256]{1,0:T(8,128)} async-done(((f32[64,256]{1,0:T(8,128)}), f32[64,256]{1,0:T(8,128)}) %all-reduce.2.cloned.1.call-update) | async-done | bytes 65552 | tf_op jit(solution)/shard_map/psum | solution.py:66
  363.0 1.5 copy.43
  (87 shorter events, 4.4 us)
Async XLA Ops:
  6.5 356.4 %all-reduce.2.cloned.1.call-start = ((), (), s32[]{:S(2)}) async-start(), calls=%async_computation | async-start | bytes 131072 | tf_op jit(solution)/shard_map/psum | solution.py:66
  16.9 20.6 %collective-permute-start.2 = (bf16[64,1536]{1,0:T(8,128)(2,1)S(1)}, bf16[64,1536]{1,0:T(8,128)(2,1)S(1)}, u32[]{:S(2)}, u32[]{:S(2)}) collective-permute-start(bf16[64,1536]{1,0:T(8,128)(2,1)S(1)} %all_gather.6), channel_id=1, source_target_pairs={{0,4},{4,8},{8,12},{12,16},{16,20},{20,24},{24,28},{28,32},{32,36}... | collective-permute-start | bytes 589832 | tf_op jit(solution)/shard_map/ppermute | solution.py:9
  16.9 39.0 %collective-permute-start.3 = (bf16[64,1536]{1,0:T(8,128)(2,1)S(1)}, bf16[64,1536]{1,0:T(8,128)(2,1)S(1)}, u32[]{:S(2)}, u32[]{:S(2)}) collective-permute-start(bf16[64,1536]{1,0:T(8,128)(2,1)S(1)} %all_gather.6), channel_id=1, source_target_pairs={{0,8},{4,12},{8,16},{12,20},{16,24},{20,28},{24,32},{28,36},{32,40... | collective-permute-start | bytes 589832 | tf_op jit(solution)/shard_map/ppermute | solution.py:9
  27.2 10.4 %collective-permute-start.5 = (bf16[64,12]{0,1:T(8,128)(2,1)S(1)}, bf16[64,12]{0,1:T(8,128)(2,1)S(1)}, u32[]{:S(2)}, u32[]{:S(2)}) collective-permute-start(bf16[64,12]{0,1:T(8,128)(2,1)S(1)} %bitcast.49), channel_id=1, source_target_pairs={{0,4},{4,8},{8,12},{12,16},{16,20},{20,24},{24,28},{28,32},{32,36}... | collective-permute-start | bytes 4616 | tf_op jit(solution)/shard_map/ppermute | solution.py:9
  30.0 25.6 %collective-permute-start.6 = (bf16[64,12]{0,1:T(8,128)(2,1)S(1)}, bf16[64,12]{0,1:T(8,128)(2,1)S(1)}, u32[]{:S(2)}, u32[]{:S(2)}) collective-permute-start(bf16[64,12]{0,1:T(8,128)(2,1)S(1)} %bitcast.50), channel_id=1, source_target_pairs={{0,8},{4,12},{8,16},{12,20},{16,24},{20,28},{24,32},{28,36},{32,40... | collective-permute-start | bytes 4616 | tf_op jit(solution)/shard_map/ppermute | solution.py:9
  37.6 18.1 %collective-permute-start.7 = (bf16[64,12]{0,1:T(8,128)(2,1)S(1)}, bf16[64,12]{0,1:T(8,128)(2,1)S(1)}, u32[]{:S(2)}, u32[]{:S(2)}) collective-permute-start(bf16[64,12]{0,1:T(8,128)(2,1)S(1)} %collective-permute-done.5), channel_id=1, source_target_pairs={{0,8},{4,12},{8,16},{12,20},{16,24},{20,28},{24,32},{28,36},{32,40... | collective-permute-start | bytes 4616 | tf_op jit(solution)/shard_map/ppermute | solution.py:9
  37.6 18.4 %collective-permute-start.4 = (bf16[64,1536]{1,0:T(8,128)(2,1)S(1)}, bf16[64,1536]{1,0:T(8,128)(2,1)S(1)}, u32[]{:S(2)}, u32[]{:S(2)}) collective-permute-start(bf16[64,1536]{1,0:T(8,128)(2,1)S(1)} %collective-permute-done.2), channel_id=1, source_target_pairs={{0,8},{4,12},{8,16},{12,20},{16,24},{20,28},{24,32},{28,36},{32,40... | collective-permute-start | bytes 589832 | tf_op jit(solution)/shard_map/ppermute | solution.py:9
  56.9 14.9 %collective-permute-start.1 = (bf16[64,1536]{1,0:T(8,128)(2,1)S(1)}, bf16[64,1536]{1,0:T(8,128)(2,1)S(1)}, u32[]{:S(2)}, u32[]{:S(2)}) collective-permute-start(bf16[64,1536]{1,0:T(8,128)(2,1)S(1)} %get-tuple-element.234), channel_id=1, source_target_pairs={{0,16},{4,20},{8,24},{12,28},{16,32},{20,36},{24,40},{28,44},{32,4... | collective-permute-start | bytes 589832 | tf_op jit(solution)/shard_map/while/body/eval_jaxpr/ppermute | solution.py:9
  59.4 12.3 %collective-permute-start = (bf16[64,12]{1,0:T(8,128)(2,1)S(1)}, bf16[64,12]{1,0:T(8,128)(2,1)S(1)}, u32[]{:S(2)}, u32[]{:S(2)}) collective-permute-start(bf16[64,12]{1,0:T(8,128)(2,1)S(1)} %get-tuple-element.235), channel_id=1, source_target_pairs={{0,16},{4,20},{8,24},{12,28},{16,32},{20,36},{24,40},{28,44},{32,4... | collective-permute-start | bytes 4616 | tf_op jit(solution)/shard_map/while/body/eval_jaxpr/ppermute | solution.py:9
  73.4 17.6 %collective-permute-start.1 = (bf16[64,1536]{1,0:T(8,128)(2,1)S(1)}, bf16[64,1536]{1,0:T(8,128)(2,1)S(1)}, u32[]{:S(2)}, u32[]{:S(2)}) collective-permute-start(bf16[64,1536]{1,0:T(8,128)(2,1)S(1)} %get-tuple-element.234), channel_id=1, source_target_pairs={{0,16},{4,20},{8,24},{12,28},{16,32},{20,36},{24,40},{28,44},{32,4... | collective-permute-start | bytes 589832 | tf_op jit(solution)/shard_map/while/body/eval_jaxpr/ppermute | solution.py:9
  74.2 16.8 %collective-permute-start = (bf16[64,12]{1,0:T(8,128)(2,1)S(1)}, bf16[64,12]{1,0:T(8,128)(2,1)S(1)}, u32[]{:S(2)}, u32[]{:S(2)}) collective-permute-start(bf16[64,12]{1,0:T(8,128)(2,1)S(1)} %get-tuple-element.235), channel_id=1, source_target_pairs={{0,16},{4,20},{8,24},{12,28},{16,32},{20,36},{24,40},{28,44},{32,4... | collective-permute-start | bytes 4616 | tf_op jit(solution)/shard_map/while/body/eval_jaxpr/ppermute | solution.py:9
  92.7 12.5 %collective-permute-start.1 = (bf16[64,1536]{1,0:T(8,128)(2,1)S(1)}, bf16[64,1536]{1,0:T(8,128)(2,1)S(1)}, u32[]{:S(2)}, u32[]{:S(2)}) collective-permute-start(bf16[64,1536]{1,0:T(8,128)(2,1)S(1)} %get-tuple-element.234), channel_id=1, source_target_pairs={{0,16},{4,20},{8,24},{12,28},{16,32},{20,36},{24,40},{28,44},{32,4... | collective-permute-start | bytes 589832 | tf_op jit(solution)/shard_map/while/body/eval_jaxpr/ppermute | solution.py:9
  92.8 12.4 %collective-permute-start = (bf16[64,12]{1,0:T(8,128)(2,1)S(1)}, bf16[64,12]{1,0:T(8,128)(2,1)S(1)}, u32[]{:S(2)}, u32[]{:S(2)}) collective-permute-start(bf16[64,12]{1,0:T(8,128)(2,1)S(1)} %get-tuple-element.235), channel_id=1, source_target_pairs={{0,16},{4,20},{8,24},{12,28},{16,32},{20,36},{24,40},{28,44},{32,4... | collective-permute-start | bytes 4616 | tf_op jit(solution)/shard_map/while/body/eval_jaxpr/ppermute | solution.py:9
  106.9 11.9 %collective-permute-start.1 = (bf16[64,1536]{1,0:T(8,128)(2,1)S(1)}, bf16[64,1536]{1,0:T(8,128)(2,1)S(1)}, u32[]{:S(2)}, u32[]{:S(2)}) collective-permute-start(bf16[64,1536]{1,0:T(8,128)(2,1)S(1)} %get-tuple-element.234), channel_id=1, source_target_pairs={{0,16},{4,20},{8,24},{12,28},{16,32},{20,36},{24,40},{28,44},{32,4... | collective-permute-start | bytes 589832 | tf_op jit(solution)/shard_map/while/body/eval_jaxpr/ppermute | solution.py:9
  107.0 11.8 %collective-permute-start = (bf16[64,12]{1,0:T(8,128)(2,1)S(1)}, bf16[64,12]{1,0:T(8,128)(2,1)S(1)}, u32[]{:S(2)}, u32[]{:S(2)}) collective-permute-start(bf16[64,12]{1,0:T(8,128)(2,1)S(1)} %get-tuple-element.235), channel_id=1, source_target_pairs={{0,16},{4,20},{8,24},{12,28},{16,32},{20,36},{24,40},{28,44},{32,4... | collective-permute-start | bytes 4616 | tf_op jit(solution)/shard_map/while/body/eval_jaxpr/ppermute | solution.py:9
  120.5 11.8 %collective-permute-start.1 = (bf16[64,1536]{1,0:T(8,128)(2,1)S(1)}, bf16[64,1536]{1,0:T(8,128)(2,1)S(1)}, u32[]{:S(2)}, u32[]{:S(2)}) collective-permute-start(bf16[64,1536]{1,0:T(8,128)(2,1)S(1)} %get-tuple-element.234), channel_id=1, source_target_pairs={{0,16},{4,20},{8,24},{12,28},{16,32},{20,36},{24,40},{28,44},{32,4... | collective-permute-start | bytes 589832 | tf_op jit(solution)/shard_map/while/body/eval_jaxpr/ppermute | solution.py:9
  120.6 11.7 %collective-permute-start = (bf16[64,12]{1,0:T(8,128)(2,1)S(1)}, bf16[64,12]{1,0:T(8,128)(2,1)S(1)}, u32[]{:S(2)}, u32[]{:S(2)}) collective-permute-start(bf16[64,12]{1,0:T(8,128)(2,1)S(1)} %get-tuple-element.235), channel_id=1, source_target_pairs={{0,16},{4,20},{8,24},{12,28},{16,32},{20,36},{24,40},{28,44},{32,4... | collective-permute-start | bytes 4616 | tf_op jit(solution)/shard_map/while/body/eval_jaxpr/ppermute | solution.py:9
  134.0 11.7 %collective-permute-start.1 = (bf16[64,1536]{1,0:T(8,128)(2,1)S(1)}, bf16[64,1536]{1,0:T(8,128)(2,1)S(1)}, u32[]{:S(2)}, u32[]{:S(2)}) collective-permute-start(bf16[64,1536]{1,0:T(8,128)(2,1)S(1)} %get-tuple-element.234), channel_id=1, source_target_pairs={{0,16},{4,20},{8,24},{12,28},{16,32},{20,36},{24,40},{28,44},{32,4... | collective-permute-start | bytes 589832 | tf_op jit(solution)/shard_map/while/body/eval_jaxpr/ppermute | solution.py:9
  134.1 11.6 %collective-permute-start = (bf16[64,12]{1,0:T(8,128)(2,1)S(1)}, bf16[64,12]{1,0:T(8,128)(2,1)S(1)}, u32[]{:S(2)}, u32[]{:S(2)}) collective-permute-start(bf16[64,12]{1,0:T(8,128)(2,1)S(1)} %get-tuple-element.235), channel_id=1, source_target_pairs={{0,16},{4,20},{8,24},{12,28},{16,32},{20,36},{24,40},{28,44},{32,4... | collective-permute-start | bytes 4616 | tf_op jit(solution)/shard_map/while/body/eval_jaxpr/ppermute | solution.py:9
  147.5 11.7 %collective-permute-start.1 = (bf16[64,1536]{1,0:T(8,128)(2,1)S(1)}, bf16[64,1536]{1,0:T(8,128)(2,1)S(1)}, u32[]{:S(2)}, u32[]{:S(2)}) collective-permute-start(bf16[64,1536]{1,0:T(8,128)(2,1)S(1)} %get-tuple-element.234), channel_id=1, source_target_pairs={{0,16},{4,20},{8,24},{12,28},{16,32},{20,36},{24,40},{28,44},{32,4... | collective-permute-start | bytes 589832 | tf_op jit(solution)/shard_map/while/body/eval_jaxpr/ppermute | solution.py:9
  147.8 11.4 %collective-permute-start = (bf16[64,12]{1,0:T(8,128)(2,1)S(1)}, bf16[64,12]{1,0:T(8,128)(2,1)S(1)}, u32[]{:S(2)}, u32[]{:S(2)}) collective-permute-start(bf16[64,12]{1,0:T(8,128)(2,1)S(1)} %get-tuple-element.235), channel_id=1, source_target_pairs={{0,16},{4,20},{8,24},{12,28},{16,32},{20,36},{24,40},{28,44},{32,4... | collective-permute-start | bytes 4616 | tf_op jit(solution)/shard_map/while/body/eval_jaxpr/ppermute | solution.py:9
  160.9 11.7 %collective-permute-start.1 = (bf16[64,1536]{1,0:T(8,128)(2,1)S(1)}, bf16[64,1536]{1,0:T(8,128)(2,1)S(1)}, u32[]{:S(2)}, u32[]{:S(2)}) collective-permute-start(bf16[64,1536]{1,0:T(8,128)(2,1)S(1)} %get-tuple-element.234), channel_id=1, source_target_pairs={{0,16},{4,20},{8,24},{12,28},{16,32},{20,36},{24,40},{28,44},{32,4... | collective-permute-start | bytes 589832 | tf_op jit(solution)/shard_map/while/body/eval_jaxpr/ppermute | solution.py:9
  162.6 10.0 %collective-permute-start = (bf16[64,12]{1,0:T(8,128)(2,1)S(1)}, bf16[64,12]{1,0:T(8,128)(2,1)S(1)}, u32[]{:S(2)}, u32[]{:S(2)}) collective-permute-start(bf16[64,12]{1,0:T(8,128)(2,1)S(1)} %get-tuple-element.235), channel_id=1, source_target_pairs={{0,16},{4,20},{8,24},{12,28},{16,32},{20,36},{24,40},{28,44},{32,4... | collective-permute-start | bytes 4616 | tf_op jit(solution)/shard_map/while/body/eval_jaxpr/ppermute | solution.py:9
  174.3 12.6 %collective-permute-start.1 = (bf16[64,1536]{1,0:T(8,128)(2,1)S(1)}, bf16[64,1536]{1,0:T(8,128)(2,1)S(1)}, u32[]{:S(2)}, u32[]{:S(2)}) collective-permute-start(bf16[64,1536]{1,0:T(8,128)(2,1)S(1)} %get-tuple-element.234), channel_id=1, source_target_pairs={{0,16},{4,20},{8,24},{12,28},{16,32},{20,36},{24,40},{28,44},{32,4... | collective-permute-start | bytes 589832 | tf_op jit(solution)/shard_map/while/body/eval_jaxpr/ppermute | solution.py:9
  175.1 11.8 %collective-permute-start = (bf16[64,12]{1,0:T(8,128)(2,1)S(1)}, bf16[64,12]{1,0:T(8,128)(2,1)S(1)}, u32[]{:S(2)}, u32[]{:S(2)}) collective-permute-start(bf16[64,12]{1,0:T(8,128)(2,1)S(1)} %get-tuple-element.235), channel_id=1, source_target_pairs={{0,16},{4,20},{8,24},{12,28},{16,32},{20,36},{24,40},{28,44},{32,4... | collective-permute-start | bytes 4616 | tf_op jit(solution)/shard_map/while/body/eval_jaxpr/ppermute | solution.py:9
  188.6 13.7 %collective-permute-start.1 = (bf16[64,1536]{1,0:T(8,128)(2,1)S(1)}, bf16[64,1536]{1,0:T(8,128)(2,1)S(1)}, u32[]{:S(2)}, u32[]{:S(2)}) collective-permute-start(bf16[64,1536]{1,0:T(8,128)(2,1)S(1)} %get-tuple-element.234), channel_id=1, source_target_pairs={{0,16},{4,20},{8,24},{12,28},{16,32},{20,36},{24,40},{28,44},{32,4... | collective-permute-start | bytes 589832 | tf_op jit(solution)/shard_map/while/body/eval_jaxpr/ppermute | solution.py:9
  188.7 13.6 %collective-permute-start = (bf16[64,12]{1,0:T(8,128)(2,1)S(1)}, bf16[64,12]{1,0:T(8,128)(2,1)S(1)}, u32[]{:S(2)}, u32[]{:S(2)}) collective-permute-start(bf16[64,12]{1,0:T(8,128)(2,1)S(1)} %get-tuple-element.235), channel_id=1, source_target_pairs={{0,16},{4,20},{8,24},{12,28},{16,32},{20,36},{24,40},{28,44},{32,4... | collective-permute-start | bytes 4616 | tf_op jit(solution)/shard_map/while/body/eval_jaxpr/ppermute | solution.py:9
  204.1 13.4 %collective-permute-start.1 = (bf16[64,1536]{1,0:T(8,128)(2,1)S(1)}, bf16[64,1536]{1,0:T(8,128)(2,1)S(1)}, u32[]{:S(2)}, u32[]{:S(2)}) collective-permute-start(bf16[64,1536]{1,0:T(8,128)(2,1)S(1)} %get-tuple-element.234), channel_id=1, source_target_pairs={{0,16},{4,20},{8,24},{12,28},{16,32},{20,36},{24,40},{28,44},{32,4... | collective-permute-start | bytes 589832 | tf_op jit(solution)/shard_map/while/body/eval_jaxpr/ppermute | solution.py:9
  204.1 13.3 %collective-permute-start = (bf16[64,12]{1,0:T(8,128)(2,1)S(1)}, bf16[64,12]{1,0:T(8,128)(2,1)S(1)}, u32[]{:S(2)}, u32[]{:S(2)}) collective-permute-start(bf16[64,12]{1,0:T(8,128)(2,1)S(1)} %get-tuple-element.235), channel_id=1, source_target_pairs={{0,16},{4,20},{8,24},{12,28},{16,32},{20,36},{24,40},{28,44},{32,4... | collective-permute-start | bytes 4616 | tf_op jit(solution)/shard_map/while/body/eval_jaxpr/ppermute | solution.py:9
  219.2 14.4 %collective-permute-start.1 = (bf16[64,1536]{1,0:T(8,128)(2,1)S(1)}, bf16[64,1536]{1,0:T(8,128)(2,1)S(1)}, u32[]{:S(2)}, u32[]{:S(2)}) collective-permute-start(bf16[64,1536]{1,0:T(8,128)(2,1)S(1)} %get-tuple-element.234), channel_id=1, source_target_pairs={{0,16},{4,20},{8,24},{12,28},{16,32},{20,36},{24,40},{28,44},{32,4... | collective-permute-start | bytes 589832 | tf_op jit(solution)/shard_map/while/body/eval_jaxpr/ppermute | solution.py:9
  219.3 14.3 %collective-permute-start = (bf16[64,12]{1,0:T(8,128)(2,1)S(1)}, bf16[64,12]{1,0:T(8,128)(2,1)S(1)}, u32[]{:S(2)}, u32[]{:S(2)}) collective-permute-start(bf16[64,12]{1,0:T(8,128)(2,1)S(1)} %get-tuple-element.235), channel_id=1, source_target_pairs={{0,16},{4,20},{8,24},{12,28},{16,32},{20,36},{24,40},{28,44},{32,4... | collective-permute-start | bytes 4616 | tf_op jit(solution)/shard_map/while/body/eval_jaxpr/ppermute | solution.py:9
  235.3 12.5 %collective-permute-start.1 = (bf16[64,1536]{1,0:T(8,128)(2,1)S(1)}, bf16[64,1536]{1,0:T(8,128)(2,1)S(1)}, u32[]{:S(2)}, u32[]{:S(2)}) collective-permute-start(bf16[64,1536]{1,0:T(8,128)(2,1)S(1)} %get-tuple-element.234), channel_id=1, source_target_pairs={{0,16},{4,20},{8,24},{12,28},{16,32},{20,36},{24,40},{28,44},{32,4... | collective-permute-start | bytes 589832 | tf_op jit(solution)/shard_map/while/body/eval_jaxpr/ppermute | solution.py:9
  235.4 12.4 %collective-permute-start = (bf16[64,12]{1,0:T(8,128)(2,1)S(1)}, bf16[64,12]{1,0:T(8,128)(2,1)S(1)}, u32[]{:S(2)}, u32[]{:S(2)}) collective-permute-start(bf16[64,12]{1,0:T(8,128)(2,1)S(1)} %get-tuple-element.235), channel_id=1, source_target_pairs={{0,16},{4,20},{8,24},{12,28},{16,32},{20,36},{24,40},{28,44},{32,4... | collective-permute-start | bytes 4616 | tf_op jit(solution)/shard_map/while/body/eval_jaxpr/ppermute | solution.py:9
  249.5 11.8 %collective-permute-start.1 = (bf16[64,1536]{1,0:T(8,128)(2,1)S(1)}, bf16[64,1536]{1,0:T(8,128)(2,1)S(1)}, u32[]{:S(2)}, u32[]{:S(2)}) collective-permute-start(bf16[64,1536]{1,0:T(8,128)(2,1)S(1)} %get-tuple-element.234), channel_id=1, source_target_pairs={{0,16},{4,20},{8,24},{12,28},{16,32},{20,36},{24,40},{28,44},{32,4... | collective-permute-start | bytes 589832 | tf_op jit(solution)/shard_map/while/body/eval_jaxpr/ppermute | solution.py:9
  249.6 11.7 %collective-permute-start = (bf16[64,12]{1,0:T(8,128)(2,1)S(1)}, bf16[64,12]{1,0:T(8,128)(2,1)S(1)}, u32[]{:S(2)}, u32[]{:S(2)}) collective-permute-start(bf16[64,12]{1,0:T(8,128)(2,1)S(1)} %get-tuple-element.235), channel_id=1, source_target_pairs={{0,16},{4,20},{8,24},{12,28},{16,32},{20,36},{24,40},{28,44},{32,4... | collective-permute-start | bytes 4616 | tf_op jit(solution)/shard_map/while/body/eval_jaxpr/ppermute | solution.py:9
  263.0 11.8 %collective-permute-start.1 = (bf16[64,1536]{1,0:T(8,128)(2,1)S(1)}, bf16[64,1536]{1,0:T(8,128)(2,1)S(1)}, u32[]{:S(2)}, u32[]{:S(2)}) collective-permute-start(bf16[64,1536]{1,0:T(8,128)(2,1)S(1)} %get-tuple-element.234), channel_id=1, source_target_pairs={{0,16},{4,20},{8,24},{12,28},{16,32},{20,36},{24,40},{28,44},{32,4... | collective-permute-start | bytes 589832 | tf_op jit(solution)/shard_map/while/body/eval_jaxpr/ppermute | solution.py:9
  263.0 11.7 %collective-permute-start = (bf16[64,12]{1,0:T(8,128)(2,1)S(1)}, bf16[64,12]{1,0:T(8,128)(2,1)S(1)}, u32[]{:S(2)}, u32[]{:S(2)}) collective-permute-start(bf16[64,12]{1,0:T(8,128)(2,1)S(1)} %get-tuple-element.235), channel_id=1, source_target_pairs={{0,16},{4,20},{8,24},{12,28},{16,32},{20,36},{24,40},{28,44},{32,4... | collective-permute-start | bytes 4616 | tf_op jit(solution)/shard_map/while/body/eval_jaxpr/ppermute | solution.py:9
  276.5 0.6 copy-start
Sparse Core Ops, SparseCore 0:
  277.2 85.6 all-reduce.1
where the time goes:
time: 372 us; the launch traced here: 371 us
  waiting for transfers between devices  239 us (64%)
  starting transfers between devices  54.3 us (15%)
  local copies, waits for them, and re-layouts  23 us (6%)
  matrix products  22.6 us (6%)
  blocking collectives  17.7 us (5%)
  between operations  13.5 us (4%)
    ppermute x36, waiting for transfers between devices, passed_along(): return lax.ppermute(x, axis, [(i, (i + by) % size) for i in range(size)])  153 us
    psum x1, waiting for transfers between devices, per_device(): product = lax.psum(running, 'team')  85.8 us
    ppermute x36, starting transfers between devices, passed_along(): return lax.ppermute(x, axis, [(i, (i + by) % size) for i in range(size)])  54.3 us
    dot_general x16, matrix products, contribute(): lax.dot_general(scaled, cov_slab, (((1,), (1,)), ((), ())), preferred_ele...  22.6 us
    unnamed x5, local copies, waits for them, and re-layouts  15.1 us
    all_gather x1, blocking collectives, per_device(): lax.all_gather(loadings, 'team', axis=1, tiled=True)  10.4 us
  transfers between devices with their start and end apart: 37, of which 17 were waited for; matrix products, arithmetic and copies ran while one was open for 5% of the time, Pallas kernels for 0%

commit v1 on v0

--- a/solution.py
+++ b/solution.py
@@ -2,6 +2,13 @@
 import jax.numpy as jnp
 from jax import lax
 from jax.sharding import PartitionSpec as P
+
+
+def exchange_gather(x, mesh_axis, dim):
+    peers = lax.axis_size(mesh_axis)
+    pieces = jnp.stack([x for _ in range(peers)])
+    pieces = lax.all_to_all(pieces, mesh_axis, split_axis=0, concat_axis=0)
+    return jnp.concatenate(pieces, axis=dim)
 
 
 def passed_along(x, axis, by):
@@ -18,7 +25,7 @@
     skew_lag = jnp.mod(cycle_pos - member, team_size)
     base_stop = jnp.mod((cycle_pos - skew_lag - member) // team_size, cycle_stops)
     held_block = (
-        lax.all_gather(loadings, "team", axis=1, tiled=True),
+        exchange_gather(loadings, "team", 1),
         lax.all_gather(scales, "team", axis=1, tiled=True),
     )
     near_copy = passed_along((held_block[0], held_block[1]), "blk", 1)

time: 372 us -> 366 us (0.984)
  starting transfers between devices: 54.3 us -> 42.3 us
    ppermute x36, waiting for transfers between devices: 153 us -> 179 us  [passed_along(): return lax.ppermute(x, axis, [(i, (i + by) % size) for i in range(size)])]
    psum x1, waiting for transfers between devices: 85.8 us -> 63.2 us  [per_device(): product = lax.psum(running, 'team')]
    ppermute x36, starting transfers between devices: 54.3 us -> 42.3 us  [passed_along(): return lax.ppermute(x, axis, [(i, (i + by) % size) for i in range(size)])]
    all_to_all x0 -> x1, blocking collectives: none -> 11.7 us  [exchange_gather(): pieces = lax.all_to_all(pieces, mesh_axis, split_axis=0, concat_axis=0)]
    all_gather x1 -> x0, blocking collectives: 10.4 us -> none  [per_device(): lax.all_gather(loadings, 'team', axis=1, tiled=True)]
  transfers between devices with their start and end apart: 37 -> 37, of which waited for: 17 -> 18; matrix products, arithmetic and copies ran while one was open for 5% -> 5% of each run, Pallas kernels for 0% -> 0%
where the time goes in v1:
time: 366 us; the launch traced here: 365 us
  waiting for transfers between devices  242 us (66%)
  starting transfers between devices  42.3 us (12%)
  local copies, waits for them, and re-layouts  24 us (7%)
  matrix products  22.5 us (6%)
  blocking collectives  19.4 us (5%)
  between operations  13.5 us (4%)
    ppermute x36, waiting for transfers between devices, passed_along(): return lax.ppermute(x, axis, [(i, (i + by) % size) for i in range(size)])  179 us
    psum x1, waiting for transfers between devices, per_device(): product = lax.psum(running, 'team')  63.2 us
    ppermute x36, starting transfers between devices, passed_along(): return lax.ppermute(x, axis, [(i, (i + by) % size) for i in range(size)])  42.3 us
    dot_general x16, matrix products, contribute(): lax.dot_general(scaled, cov_slab, (((1,), (1,)), ((), ())), preferred_ele...  22.5 us
    unnamed x5, local copies, waits for them, and re-layouts  15.1 us
    all_to_all x1, blocking collectives, exchange_gather(): pieces = lax.all_to_all(pieces, mesh_axis, split_axis=0, concat_axis=0)  11.7 us
    all_gather x1, blocking collectives, per_device(): lax.all_gather(scales, 'team', axis=1, tiled=True)  7.65 us
  transfers between devices with their start and end apart: 37, of which 18 were waited for; matrix products, arithmetic and copies ran while one was open for 5% of the time, Pallas kernels for 0%

profile of v1, /device:TPU:1, one launch (start us, length us, event | category | flops | bytes accessed | tf_op | source)
XLA Modules:
  0.0 365.0 jit_solution(18233982713644026447)
XLA Ops:
  6.5 0.8 stack.34
  7.4 11.7 %all_to_all.5 = bf16[4,64,384]{2,1,0:T(8,128)(2,1)S(1)} all-to-all(bf16[4,64,384]{2,1,0:T(8,128)(2,1)S(1)} %stack.34), channel_id=1, replica_groups=mesh['blk'=64,'team'=4] {'team'}, dimensions={0} | all-to-all | bytes 393216 | tf_op jit(solution)/shard_map/all_to_all | solution.py:10
  19.1 1.7 collective-permute-start.2
  20.8 7.7 %all-gather = bf16[4,3,64]{2,1,0:T(4,128)(2,1)S(1)} all-gather(bf16[1,3,64]{2,1,0:T(4,128)(2,1)} %bitcast.60), channel_id=1, replica_groups=mesh['blk'=64,'team'=4] {'team'}, dimensions={0}, use_global_device_ids=true | all-gather | bytes 1920 | tf_op jit(solution)/shard_map/all_gather | solution.py:29
  28.5 1.7 collective-permute-start.5
  30.1 4.2 %collective-permute-start.6 = (bf16[64,12]{0,1:T(8,128)(2,1)S(1)}, bf16[64,12]{0,1:T(8,128)(2,1)S(1)}, u32[]{:S(2)}, u32[]{:S(2)}) collective-permute-start(bf16[64,12]{0,1:T(8,128)(2,1)S(1)} %bitcast.55), channel_id=1, source_target_pairs={{0,8},{4,12},{8,16},{12,20},{16,24},{20,28},{24,32},{28,36},{32,40... | collective-permute-start | bytes 4616 | tf_op jit(solution)/shard_map/ppermute | solution.py:16
  34.3 1.3 collective-permute-done.5
  35.6 2.8 collective-permute-start.3
  38.5 4.4 %constant_dynamic-slice_fusion = bf16[256,1,1,1536]{3,1,2,0:T(2,128)(2,1)S(1)} fusion(bf16[256,16,1,1536]{3,1,2,0:T(8,128)(2,1)} %param.7, s32[]{:T(128)S(6)} %select_n.61), kind=kLoop, calls=%fused_computation.27 | loop fusion | bytes 1572868 | tf_op jit(solution)/shard_map/jit(dynamic_index_in_dim)/dynamic_slice | solution.py:56
  42.9 13.0 %copy.34 = bf16[256,16,1,1536]{3,0,1,2:T(8,128)(2,1)} copy(bf16[256,16,1,1536]{3,1,2,0:T(8,128)(2,1)} %param.7) | data formatting | bytes 25165824 | tf_op args[2]
  56.4 3.5 collective-permute-done.4
  60.2 0.2 multiply_convert_fusion
  60.4 0.4 fusion.5
  60.8 232.1 %while.19 = (s32[]{:T(128)}, f32[64,256]{1,0:T(8,128)S(1)}, bf16[64,1536]{1,0:T(8,128)(2,1)S(1)}, bf16[64,12]{1,0:T(8,128)(2,1)S(1)}, s32[]{:T(128)}, /*index=5*...) while((s32[]{:T(128)}, f32[64,256]{1,0:T(8,128)S(1)}, ...), condition=%wide.region_1.2_spmd, body=%wide.region_0.1_spmd.sunk | while | flops 50642960 | bytes 3091284 | solution.py:72
  60.9 2.7 collective-permute-start
  63.6 14.7 %collective-permute-done = bf16[64,12]{1,0:T(8,128)(2,1)S(1)} collective-permute-done((bf16[64,12]{1,0:T(8,128)(2,1)S(1)}, bf16[64,12]{1,0:T(8,128)(2,1)S(1)}, u32[]{:S(2)}, u32[]{:S(2)}) %collective-permute-start) | collective-permute-done | bytes 1568 | tf_op jit(solution)/shard_map/while/body/eval_jaxpr/ppermute | solution.py:16
  78.3 0.2 mul.51
  78.5 1.5 convolution_add_fusion.2
  80.2 16.7 %collective-permute-done = bf16[64,12]{1,0:T(8,128)(2,1)S(1)} collective-permute-done((bf16[64,12]{1,0:T(8,128)(2,1)S(1)}, bf16[64,12]{1,0:T(8,128)(2,1)S(1)}, u32[]{:S(2)}, u32[]{:S(2)}) %collective-permute-start) | collective-permute-done | bytes 1568 | tf_op jit(solution)/shard_map/while/body/eval_jaxpr/ppermute | solution.py:16
  97.2 1.5 convolution_add_fusion.2
  98.9 13.0 %collective-permute-done = bf16[64,12]{1,0:T(8,128)(2,1)S(1)} collective-permute-done((bf16[64,12]{1,0:T(8,128)(2,1)S(1)}, bf16[64,12]{1,0:T(8,128)(2,1)S(1)}, u32[]{:S(2)}, u32[]{:S(2)}) %collective-permute-start) | collective-permute-done | bytes 1568 | tf_op jit(solution)/shard_map/while/body/eval_jaxpr/ppermute | solution.py:16
  112.1 1.5 convolution_add_fusion.2
  113.6 1.1 collective-permute-start.1
  114.9 11.1 %collective-permute-done = bf16[64,12]{1,0:T(8,128)(2,1)S(1)} collective-permute-done((bf16[64,12]{1,0:T(8,128)(2,1)S(1)}, bf16[64,12]{1,0:T(8,128)(2,1)S(1)}, u32[]{:S(2)}, u32[]{:S(2)}) %collective-permute-start) | collective-permute-done | bytes 1568 | tf_op jit(solution)/shard_map/while/body/eval_jaxpr/ppermute | solution.py:16
  126.2 1.5 convolution_add_fusion.2
  127.7 0.8 collective-permute-start.1
  128.4 1.5 collective-permute-start
  129.9 9.5 %collective-permute-done = bf16[64,12]{1,0:T(8,128)(2,1)S(1)} collective-permute-done((bf16[64,12]{1,0:T(8,128)(2,1)S(1)}, bf16[64,12]{1,0:T(8,128)(2,1)S(1)}, u32[]{:S(2)}, u32[]{:S(2)}) %collective-permute-start) | collective-permute-done | bytes 1568 | tf_op jit(solution)/shard_map/while/body/eval_jaxpr/ppermute | solution.py:16
  139.6 1.5 convolution_add_fusion.2
  141.1 1.8 collective-permute-start.1
  142.9 1.0 collective-permute-start
  143.9 9.0 %collective-permute-done = bf16[64,12]{1,0:T(8,128)(2,1)S(1)} collective-permute-done((bf16[64,12]{1,0:T(8,128)(2,1)S(1)}, bf16[64,12]{1,0:T(8,128)(2,1)S(1)}, u32[]{:S(2)}, u32[]{:S(2)}) %collective-permute-start) | collective-permute-done | bytes 1568 | tf_op jit(solution)/shard_map/while/body/eval_jaxpr/ppermute | solution.py:16
  153.2 1.5 convolution_add_fusion.2
  154.7 5.0 %collective-permute-start = (bf16[64,12]{1,0:T(8,128)(2,1)S(1)}, bf16[64,12]{1,0:T(8,128)(2,1)S(1)}, u32[]{:S(2)}, u32[]{:S(2)}) collective-permute-start(bf16[64,12]{1,0:T(8,128)(2,1)S(1)} %get-tuple-element.241), channel_id=1, source_target_pairs={{0,16},{4,20},{8,24},{12,28},{16,32},{20,36},{24,40},{28,44},{32,4... | collective-permute-start | bytes 4616 | tf_op jit(solution)/shard_map/while/body/eval_jaxpr/ppermute | solution.py:16
  159.7 6.6 %collective-permute-done = bf16[64,12]{1,0:T(8,128)(2,1)S(1)} collective-permute-done((bf16[64,12]{1,0:T(8,128)(2,1)S(1)}, bf16[64,12]{1,0:T(8,128)(2,1)S(1)}, u32[]{:S(2)}, u32[]{:S(2)}) %collective-permute-start) | collective-permute-done | bytes 1568 | tf_op jit(solution)/shard_map/while/body/eval_jaxpr/ppermute | solution.py:16
  166.6 1.5 convolution_add_fusion.2
  168.1 0.4 collective-permute-start.1
  168.5 6.1 %collective-permute-start = (bf16[64,12]{1,0:T(8,128)(2,1)S(1)}, bf16[64,12]{1,0:T(8,128)(2,1)S(1)}, u32[]{:S(2)}, u32[]{:S(2)}) collective-permute-start(bf16[64,12]{1,0:T(8,128)(2,1)S(1)} %get-tuple-element.241), channel_id=1, source_target_pairs={{0,16},{4,20},{8,24},{12,28},{16,32},{20,36},{24,40},{28,44},{32,4... | collective-permute-start | bytes 4616 | tf_op jit(solution)/shard_map/while/body/eval_jaxpr/ppermute | solution.py:16
  174.6 5.6 %collective-permute-done = bf16[64,12]{1,0:T(8,128)(2,1)S(1)} collective-permute-done((bf16[64,12]{1,0:T(8,128)(2,1)S(1)}, bf16[64,12]{1,0:T(8,128)(2,1)S(1)}, u32[]{:S(2)}, u32[]{:S(2)}) %collective-permute-start) | collective-permute-done | bytes 1568 | tf_op jit(solution)/shard_map/while/body/eval_jaxpr/ppermute | solution.py:16
  180.5 1.5 convolution_add_fusion.2
  182.0 1.4 collective-permute-start.1
  183.4 3.0 collective-permute-start
  186.4 7.3 %collective-permute-done = bf16[64,12]{1,0:T(8,128)(2,1)S(1)} collective-permute-done((bf16[64,12]{1,0:T(8,128)(2,1)S(1)}, bf16[64,12]{1,0:T(8,128)(2,1)S(1)}, u32[]{:S(2)}, u32[]{:S(2)}) %collective-permute-start) | collective-permute-done | bytes 1568 | tf_op jit(solution)/shard_map/while/body/eval_jaxpr/ppermute | solution.py:16
  193.9 1.5 convolution_add_fusion.2
  195.4 0.5 collective-permute-start.1
  195.9 1.8 collective-permute-start
  197.7 9.7 %collective-permute-done = bf16[64,12]{1,0:T(8,128)(2,1)S(1)} collective-permute-done((bf16[64,12]{1,0:T(8,128)(2,1)S(1)}, bf16[64,12]{1,0:T(8,128)(2,1)S(1)}, u32[]{:S(2)}, u32[]{:S(2)}) %collective-permute-start) | collective-permute-done | bytes 1568 | tf_op jit(solution)/shard_map/while/body/eval_jaxpr/ppermute | solution.py:16
  207.6 1.5 convolution_add_fusion.2
  209.1 2.3 collective-permute-start
  211.4 10.6 %collective-permute-done = bf16[64,12]{1,0:T(8,128)(2,1)S(1)} collective-permute-done((bf16[64,12]{1,0:T(8,128)(2,1)S(1)}, bf16[64,12]{1,0:T(8,128)(2,1)S(1)}, u32[]{:S(2)}, u32[]{:S(2)}) %collective-permute-start) | collective-permute-done | bytes 1568 | tf_op jit(solution)/shard_map/while/body/eval_jaxpr/ppermute | solution.py:16
  222.3 1.5 convolution_add_fusion.2
  223.9 0.8 collective-permute-start
  224.7 13.7 %collective-permute-done = bf16[64,12]{1,0:T(8,128)(2,1)S(1)} collective-permute-done((bf16[64,12]{1,0:T(8,128)(2,1)S(1)}, bf16[64,12]{1,0:T(8,128)(2,1)S(1)}, u32[]{:S(2)}, u32[]{:S(2)}) %collective-permute-start) | collective-permute-done | bytes 1568 | tf_op jit(solution)/shard_map/while/body/eval_jaxpr/ppermute | solution.py:16
  238.6 1.5 convolution_add_fusion.2
  240.3 14.7 %collective-permute-done = bf16[64,12]{1,0:T(8,128)(2,1)S(1)} collective-permute-done((bf16[64,12]{1,0:T(8,128)(2,1)S(1)}, bf16[64,12]{1,0:T(8,128)(2,1)S(1)}, u32[]{:S(2)}, u32[]{:S(2)}) %collective-permute-start) | collective-permute-done | bytes 1568 | tf_op jit(solution)/shard_map/while/body/eval_jaxpr/ppermute | solution.py:16
  255.3 1.5 convolution_add_fusion.2
  256.8 0.4 collective-permute-start.1
  257.2 16.0 %collective-permute-done = bf16[64,12]{1,0:T(8,128)(2,1)S(1)} collective-permute-done((bf16[64,12]{1,0:T(8,128)(2,1)S(1)}, bf16[64,12]{1,0:T(8,128)(2,1)S(1)}, u32[]{:S(2)}, u32[]{:S(2)}) %collective-permute-start) | collective-permute-done | bytes 1568 | tf_op jit(solution)/shard_map/while/body/eval_jaxpr/ppermute | solution.py:16
  273.4 1.5 convolution_add_fusion.2
  275.1 16.0 %collective-permute-done = bf16[64,12]{1,0:T(8,128)(2,1)S(1)} collective-permute-done((bf16[64,12]{1,0:T(8,128)(2,1)S(1)}, bf16[64,12]{1,0:T(8,128)(2,1)S(1)}, u32[]{:S(2)}, u32[]{:S(2)}) %collective-permute-start) | collective-permute-done | bytes 1568 | tf_op jit(solution)/shard_map/while/body/eval_jaxpr/ppermute | solution.py:16
  291.4 1.5 convolution_add_fusion.2
  292.9 0.6 copy-done
  293.5 63.2 %all-reduce.2.cloned.1.call-done = f32[64,256]{1,0:T(8,128)} async-done(((f32[64,256]{1,0:T(8,128)}), f32[64,256]{1,0:T(8,128)}) %all-reduce.2.cloned.1.call-update) | async-done | bytes 65552 | tf_op jit(solution)/shard_map/psum | solution.py:73
  356.7 1.5 copy.50
  (91 shorter events, 5.0 us)
Async XLA Ops:
  6.5 350.2 %all-reduce.2.cloned.1.call-start = ((), (), s32[]{:S(2)}) async-start(), calls=%async_computation.1 | async-start | bytes 131072 | tf_op jit(solution)/shard_map/psum | solution.py:73
  19.1 19.4 %collective-permute-start.2 = (bf16[64,1536]{1,0:T(8,128)(2,1)S(1)}, bf16[64,1536]{1,0:T(8,128)(2,1)S(1)}, u32[]{:S(2)}, u32[]{:S(2)}) collective-permute-start(bf16[64,1536]{1,0:T(8,128)(2,1)S(1)} %bitcast.52), channel_id=1, source_target_pairs={{0,4},{4,8},{8,12},{12,16},{16,20},{20,24},{24,28},{28,32},{32,36}... | collective-permute-start | bytes 589832 | tf_op jit(solution)/shard_map/ppermute | solution.py:16
  28.5 7.2 %collective-permute-start.5 = (bf16[64,12]{0,1:T(8,128)(2,1)S(1)}, bf16[64,12]{0,1:T(8,128)(2,1)S(1)}, u32[]{:S(2)}, u32[]{:S(2)}) collective-permute-start(bf16[64,12]{0,1:T(8,128)(2,1)S(1)} %bitcast.54), channel_id=1, source_target_pairs={{0,4},{4,8},{8,12},{12,16},{16,20},{20,24},{24,28},{28,32},{32,36}... | collective-permute-start | bytes 4616 | tf_op jit(solution)/shard_map/ppermute | solution.py:16
  30.1 25.8 %collective-permute-start.6 = (bf16[64,12]{0,1:T(8,128)(2,1)S(1)}, bf16[64,12]{0,1:T(8,128)(2,1)S(1)}, u32[]{:S(2)}, u32[]{:S(2)}) collective-permute-start(bf16[64,12]{0,1:T(8,128)(2,1)S(1)} %bitcast.55), channel_id=1, source_target_pairs={{0,8},{4,12},{8,16},{12,20},{16,24},{20,28},{24,32},{28,36},{32,40... | collective-permute-start | bytes 4616 | tf_op jit(solution)/shard_map/ppermute | solution.py:16
  35.6 20.3 %collective-permute-start.7 = (bf16[64,12]{0,1:T(8,128)(2,1)S(1)}, bf16[64,12]{0,1:T(8,128)(2,1)S(1)}, u32[]{:S(2)}, u32[]{:S(2)}) collective-permute-start(bf16[64,12]{0,1:T(8,128)(2,1)S(1)} %collective-permute-done.5), channel_id=1, source_target_pairs={{0,8},{4,12},{8,16},{12,20},{16,24},{20,28},{24,32},{28,36},{32,40... | collective-permute-start | bytes 4616 | tf_op jit(solution)/shard_map/ppermute | solution.py:16
  35.6 20.8 %collective-permute-start.3 = (bf16[64,1536]{1,0:T(8,128)(2,1)S(1)}, bf16[64,1536]{1,0:T(8,128)(2,1)S(1)}, u32[]{:S(2)}, u32[]{:S(2)}) collective-permute-start(bf16[64,1536]{1,0:T(8,128)(2,1)S(1)} %bitcast.53), channel_id=1, source_target_pairs={{0,8},{4,12},{8,16},{12,20},{16,24},{20,28},{24,32},{28,36},{32,40... | collective-permute-start | bytes 589832 | tf_op jit(solution)/shard_map/ppermute | solution.py:16
  38.4 21.5 %collective-permute-start.4 = (bf16[64,1536]{1,0:T(8,128)(2,1)S(1)}, bf16[64,1536]{1,0:T(8,128)(2,1)S(1)}, u32[]{:S(2)}, u32[]{:S(2)}) collective-permute-start(bf16[64,1536]{1,0:T(8,128)(2,1)S(1)} %collective-permute-done.2), channel_id=1, source_target_pairs={{0,8},{4,12},{8,16},{12,20},{16,24},{20,28},{24,32},{28,36},{32,40... | collective-permute-start | bytes 589832 | tf_op jit(solution)/shard_map/ppermute | solution.py:16
  60.8 17.5 %collective-permute-start.1 = (bf16[64,1536]{1,0:T(8,128)(2,1)S(1)}, bf16[64,1536]{1,0:T(8,128)(2,1)S(1)}, u32[]{:S(2)}, u32[]{:S(2)}) collective-permute-start(bf16[64,1536]{1,0:T(8,128)(2,1)S(1)} %get-tuple-element.240), channel_id=1, source_target_pairs={{0,16},{4,20},{8,24},{12,28},{16,32},{20,36},{24,40},{28,44},{32,4... | collective-permute-start | bytes 589832 | tf_op jit(solution)/shard_map/while/body/eval_jaxpr/ppermute | solution.py:16
  60.9 17.4 %collective-permute-start = (bf16[64,12]{1,0:T(8,128)(2,1)S(1)}, bf16[64,12]{1,0:T(8,128)(2,1)S(1)}, u32[]{:S(2)}, u32[]{:S(2)}) collective-permute-start(bf16[64,12]{1,0:T(8,128)(2,1)S(1)} %get-tuple-element.241), channel_id=1, source_target_pairs={{0,16},{4,20},{8,24},{12,28},{16,32},{20,36},{24,40},{28,44},{32,4... | collective-permute-start | bytes 4616 | tf_op jit(solution)/shard_map/while/body/eval_jaxpr/ppermute | solution.py:16
  80.0 17.0 %collective-permute-start.1 = (bf16[64,1536]{1,0:T(8,128)(2,1)S(1)}, bf16[64,1536]{1,0:T(8,128)(2,1)S(1)}, u32[]{:S(2)}, u32[]{:S(2)}) collective-permute-start(bf16[64,1536]{1,0:T(8,128)(2,1)S(1)} %get-tuple-element.240), channel_id=1, source_target_pairs={{0,16},{4,20},{8,24},{12,28},{16,32},{20,36},{24,40},{28,44},{32,4... | collective-permute-start | bytes 589832 | tf_op jit(solution)/shard_map/while/body/eval_jaxpr/ppermute | solution.py:16
  80.1 16.9 %collective-permute-start = (bf16[64,12]{1,0:T(8,128)(2,1)S(1)}, bf16[64,12]{1,0:T(8,128)(2,1)S(1)}, u32[]{:S(2)}, u32[]{:S(2)}) collective-permute-start(bf16[64,12]{1,0:T(8,128)(2,1)S(1)} %get-tuple-element.241), channel_id=1, source_target_pairs={{0,16},{4,20},{8,24},{12,28},{16,32},{20,36},{24,40},{28,44},{32,4... | collective-permute-start | bytes 4616 | tf_op jit(solution)/shard_map/while/body/eval_jaxpr/ppermute | solution.py:16
  98.7 13.2 %collective-permute-start.1 = (bf16[64,1536]{1,0:T(8,128)(2,1)S(1)}, bf16[64,1536]{1,0:T(8,128)(2,1)S(1)}, u32[]{:S(2)}, u32[]{:S(2)}) collective-permute-start(bf16[64,1536]{1,0:T(8,128)(2,1)S(1)} %get-tuple-element.240), channel_id=1, source_target_pairs={{0,16},{4,20},{8,24},{12,28},{16,32},{20,36},{24,40},{28,44},{32,4... | collective-permute-start | bytes 589832 | tf_op jit(solution)/shard_map/while/body/eval_jaxpr/ppermute | solution.py:16
  98.8 13.1 %collective-permute-start = (bf16[64,12]{1,0:T(8,128)(2,1)S(1)}, bf16[64,12]{1,0:T(8,128)(2,1)S(1)}, u32[]{:S(2)}, u32[]{:S(2)}) collective-permute-start(bf16[64,12]{1,0:T(8,128)(2,1)S(1)} %get-tuple-element.241), channel_id=1, source_target_pairs={{0,16},{4,20},{8,24},{12,28},{16,32},{20,36},{24,40},{28,44},{32,4... | collective-permute-start | bytes 4616 | tf_op jit(solution)/shard_map/while/body/eval_jaxpr/ppermute | solution.py:16
  113.6 12.3 %collective-permute-start.1 = (bf16[64,1536]{1,0:T(8,128)(2,1)S(1)}, bf16[64,1536]{1,0:T(8,128)(2,1)S(1)}, u32[]{:S(2)}, u32[]{:S(2)}) collective-permute-start(bf16[64,1536]{1,0:T(8,128)(2,1)S(1)} %get-tuple-element.240), channel_id=1, source_target_pairs={{0,16},{4,20},{8,24},{12,28},{16,32},{20,36},{24,40},{28,44},{32,4... | collective-permute-start | bytes 589832 | tf_op jit(solution)/shard_map/while/body/eval_jaxpr/ppermute | solution.py:16
  114.8 11.2 %collective-permute-start = (bf16[64,12]{1,0:T(8,128)(2,1)S(1)}, bf16[64,12]{1,0:T(8,128)(2,1)S(1)}, u32[]{:S(2)}, u32[]{:S(2)}) collective-permute-start(bf16[64,12]{1,0:T(8,128)(2,1)S(1)} %get-tuple-element.241), channel_id=1, source_target_pairs={{0,16},{4,20},{8,24},{12,28},{16,32},{20,36},{24,40},{28,44},{32,4... | collective-permute-start | bytes 4616 | tf_op jit(solution)/shard_map/while/body/eval_jaxpr/ppermute | solution.py:16
  127.7 11.7 %collective-permute-start.1 = (bf16[64,1536]{1,0:T(8,128)(2,1)S(1)}, bf16[64,1536]{1,0:T(8,128)(2,1)S(1)}, u32[]{:S(2)}, u32[]{:S(2)}) collective-permute-start(bf16[64,1536]{1,0:T(8,128)(2,1)S(1)} %get-tuple-element.240), channel_id=1, source_target_pairs={{0,16},{4,20},{8,24},{12,28},{16,32},{20,36},{24,40},{28,44},{32,4... | collective-permute-start | bytes 589832 | tf_op jit(solution)/shard_map/while/body/eval_jaxpr/ppermute | solution.py:16
  128.4 10.9 %collective-permute-start = (bf16[64,12]{1,0:T(8,128)(2,1)S(1)}, bf16[64,12]{1,0:T(8,128)(2,1)S(1)}, u32[]{:S(2)}, u32[]{:S(2)}) collective-permute-start(bf16[64,12]{1,0:T(8,128)(2,1)S(1)} %get-tuple-element.241), channel_id=1, source_target_pairs={{0,16},{4,20},{8,24},{12,28},{16,32},{20,36},{24,40},{28,44},{32,4... | collective-permute-start | bytes 4616 | tf_op jit(solution)/shard_map/while/body/eval_jaxpr/ppermute | solution.py:16
  141.1 11.9 %collective-permute-start.1 = (bf16[64,1536]{1,0:T(8,128)(2,1)S(1)}, bf16[64,1536]{1,0:T(8,128)(2,1)S(1)}, u32[]{:S(2)}, u32[]{:S(2)}) collective-permute-start(bf16[64,1536]{1,0:T(8,128)(2,1)S(1)} %get-tuple-element.240), channel_id=1, source_target_pairs={{0,16},{4,20},{8,24},{12,28},{16,32},{20,36},{24,40},{28,44},{32,4... | collective-permute-start | bytes 589832 | tf_op jit(solution)/shard_map/while/body/eval_jaxpr/ppermute | solution.py:16
  142.9 10.1 %collective-permute-start = (bf16[64,12]{1,0:T(8,128)(2,1)S(1)}, bf16[64,12]{1,0:T(8,128)(2,1)S(1)}, u32[]{:S(2)}, u32[]{:S(2)}) collective-permute-start(bf16[64,12]{1,0:T(8,128)(2,1)S(1)} %get-tuple-element.241), channel_id=1, source_target_pairs={{0,16},{4,20},{8,24},{12,28},{16,32},{20,36},{24,40},{28,44},{32,4... | collective-permute-start | bytes 4616 | tf_op jit(solution)/shard_map/while/body/eval_jaxpr/ppermute | solution.py:16
  154.6 11.7 %collective-permute-start.1 = (bf16[64,1536]{1,0:T(8,128)(2,1)S(1)}, bf16[64,1536]{1,0:T(8,128)(2,1)S(1)}, u32[]{:S(2)}, u32[]{:S(2)}) collective-permute-start(bf16[64,1536]{1,0:T(8,128)(2,1)S(1)} %get-tuple-element.240), channel_id=1, source_target_pairs={{0,16},{4,20},{8,24},{12,28},{16,32},{20,36},{24,40},{28,44},{32,4... | collective-permute-start | bytes 589832 | tf_op jit(solution)/shard_map/while/body/eval_jaxpr/ppermute | solution.py:16
  154.7 11.6 %collective-permute-start = (bf16[64,12]{1,0:T(8,128)(2,1)S(1)}, bf16[64,12]{1,0:T(8,128)(2,1)S(1)}, u32[]{:S(2)}, u32[]{:S(2)}) collective-permute-start(bf16[64,12]{1,0:T(8,128)(2,1)S(1)} %get-tuple-element.241), channel_id=1, source_target_pairs={{0,16},{4,20},{8,24},{12,28},{16,32},{20,36},{24,40},{28,44},{32,4... | collective-permute-start | bytes 4616 | tf_op jit(solution)/shard_map/while/body/eval_jaxpr/ppermute | solution.py:16
  168.1 12.2 %collective-permute-start.1 = (bf16[64,1536]{1,0:T(8,128)(2,1)S(1)}, bf16[64,1536]{1,0:T(8,128)(2,1)S(1)}, u32[]{:S(2)}, u32[]{:S(2)}) collective-permute-start(bf16[64,1536]{1,0:T(8,128)(2,1)S(1)} %get-tuple-element.240), channel_id=1, source_target_pairs={{0,16},{4,20},{8,24},{12,28},{16,32},{20,36},{24,40},{28,44},{32,4... | collective-permute-start | bytes 589832 | tf_op jit(solution)/shard_map/while/body/eval_jaxpr/ppermute | solution.py:16
  168.5 11.8 %collective-permute-start = (bf16[64,12]{1,0:T(8,128)(2,1)S(1)}, bf16[64,12]{1,0:T(8,128)(2,1)S(1)}, u32[]{:S(2)}, u32[]{:S(2)}) collective-permute-start(bf16[64,12]{1,0:T(8,128)(2,1)S(1)} %get-tuple-element.241), channel_id=1, source_target_pairs={{0,16},{4,20},{8,24},{12,28},{16,32},{20,36},{24,40},{28,44},{32,4... | collective-permute-start | bytes 4616 | tf_op jit(solution)/shard_map/while/body/eval_jaxpr/ppermute | solution.py:16
  182.0 11.7 %collective-permute-start.1 = (bf16[64,1536]{1,0:T(8,128)(2,1)S(1)}, bf16[64,1536]{1,0:T(8,128)(2,1)S(1)}, u32[]{:S(2)}, u32[]{:S(2)}) collective-permute-start(bf16[64,1536]{1,0:T(8,128)(2,1)S(1)} %get-tuple-element.240), channel_id=1, source_target_pairs={{0,16},{4,20},{8,24},{12,28},{16,32},{20,36},{24,40},{28,44},{32,4... | collective-permute-start | bytes 589832 | tf_op jit(solution)/shard_map/while/body/eval_jaxpr/ppermute | solution.py:16
  183.4 10.3 %collective-permute-start = (bf16[64,12]{1,0:T(8,128)(2,1)S(1)}, bf16[64,12]{1,0:T(8,128)(2,1)S(1)}, u32[]{:S(2)}, u32[]{:S(2)}) collective-permute-start(bf16[64,12]{1,0:T(8,128)(2,1)S(1)} %get-tuple-element.241), channel_id=1, source_target_pairs={{0,16},{4,20},{8,24},{12,28},{16,32},{20,36},{24,40},{28,44},{32,4... | collective-permute-start | bytes 4616 | tf_op jit(solution)/shard_map/while/body/eval_jaxpr/ppermute | solution.py:16
  195.4 12.0 %collective-permute-start.1 = (bf16[64,1536]{1,0:T(8,128)(2,1)S(1)}, bf16[64,1536]{1,0:T(8,128)(2,1)S(1)}, u32[]{:S(2)}, u32[]{:S(2)}) collective-permute-start(bf16[64,1536]{1,0:T(8,128)(2,1)S(1)} %get-tuple-element.240), channel_id=1, source_target_pairs={{0,16},{4,20},{8,24},{12,28},{16,32},{20,36},{24,40},{28,44},{32,4... | collective-permute-start | bytes 589832 | tf_op jit(solution)/shard_map/while/body/eval_jaxpr/ppermute | solution.py:16
  195.9 11.4 %collective-permute-start = (bf16[64,12]{1,0:T(8,128)(2,1)S(1)}, bf16[64,12]{1,0:T(8,128)(2,1)S(1)}, u32[]{:S(2)}, u32[]{:S(2)}) collective-permute-start(bf16[64,12]{1,0:T(8,128)(2,1)S(1)} %get-tuple-element.241), channel_id=1, source_target_pairs={{0,16},{4,20},{8,24},{12,28},{16,32},{20,36},{24,40},{28,44},{32,4... | collective-permute-start | bytes 4616 | tf_op jit(solution)/shard_map/while/body/eval_jaxpr/ppermute | solution.py:16
  209.1 13.0 %collective-permute-start.1 = (bf16[64,1536]{1,0:T(8,128)(2,1)S(1)}, bf16[64,1536]{1,0:T(8,128)(2,1)S(1)}, u32[]{:S(2)}, u32[]{:S(2)}) collective-permute-start(bf16[64,1536]{1,0:T(8,128)(2,1)S(1)} %get-tuple-element.240), channel_id=1, source_target_pairs={{0,16},{4,20},{8,24},{12,28},{16,32},{20,36},{24,40},{28,44},{32,4... | collective-permute-start | bytes 589832 | tf_op jit(solution)/shard_map/while/body/eval_jaxpr/ppermute | solution.py:16
  209.1 12.9 %collective-permute-start = (bf16[64,12]{1,0:T(8,128)(2,1)S(1)}, bf16[64,12]{1,0:T(8,128)(2,1)S(1)}, u32[]{:S(2)}, u32[]{:S(2)}) collective-permute-start(bf16[64,12]{1,0:T(8,128)(2,1)S(1)} %get-tuple-element.241), channel_id=1, source_target_pairs={{0,16},{4,20},{8,24},{12,28},{16,32},{20,36},{24,40},{28,44},{32,4... | collective-permute-start | bytes 4616 | tf_op jit(solution)/shard_map/while/body/eval_jaxpr/ppermute | solution.py:16
  223.8 14.6 %collective-permute-start.1 = (bf16[64,1536]{1,0:T(8,128)(2,1)S(1)}, bf16[64,1536]{1,0:T(8,128)(2,1)S(1)}, u32[]{:S(2)}, u32[]{:S(2)}) collective-permute-start(bf16[64,1536]{1,0:T(8,128)(2,1)S(1)} %get-tuple-element.240), channel_id=1, source_target_pairs={{0,16},{4,20},{8,24},{12,28},{16,32},{20,36},{24,40},{28,44},{32,4... | collective-permute-start | bytes 589832 | tf_op jit(solution)/shard_map/while/body/eval_jaxpr/ppermute | solution.py:16
  223.9 14.5 %collective-permute-start = (bf16[64,12]{1,0:T(8,128)(2,1)S(1)}, bf16[64,12]{1,0:T(8,128)(2,1)S(1)}, u32[]{:S(2)}, u32[]{:S(2)}) collective-permute-start(bf16[64,12]{1,0:T(8,128)(2,1)S(1)} %get-tuple-element.241), channel_id=1, source_target_pairs={{0,16},{4,20},{8,24},{12,28},{16,32},{20,36},{24,40},{28,44},{32,4... | collective-permute-start | bytes 4616 | tf_op jit(solution)/shard_map/while/body/eval_jaxpr/ppermute | solution.py:16
  240.1 14.9 %collective-permute-start.1 = (bf16[64,1536]{1,0:T(8,128)(2,1)S(1)}, bf16[64,1536]{1,0:T(8,128)(2,1)S(1)}, u32[]{:S(2)}, u32[]{:S(2)}) collective-permute-start(bf16[64,1536]{1,0:T(8,128)(2,1)S(1)} %get-tuple-element.240), channel_id=1, source_target_pairs={{0,16},{4,20},{8,24},{12,28},{16,32},{20,36},{24,40},{28,44},{32,4... | collective-permute-start | bytes 589832 | tf_op jit(solution)/shard_map/while/body/eval_jaxpr/ppermute | solution.py:16
  240.2 14.8 %collective-permute-start = (bf16[64,12]{1,0:T(8,128)(2,1)S(1)}, bf16[64,12]{1,0:T(8,128)(2,1)S(1)}, u32[]{:S(2)}, u32[]{:S(2)}) collective-permute-start(bf16[64,12]{1,0:T(8,128)(2,1)S(1)} %get-tuple-element.241), channel_id=1, source_target_pairs={{0,16},{4,20},{8,24},{12,28},{16,32},{20,36},{24,40},{28,44},{32,4... | collective-permute-start | bytes 4616 | tf_op jit(solution)/shard_map/while/body/eval_jaxpr/ppermute | solution.py:16
  256.8 16.5 %collective-permute-start.1 = (bf16[64,1536]{1,0:T(8,128)(2,1)S(1)}, bf16[64,1536]{1,0:T(8,128)(2,1)S(1)}, u32[]{:S(2)}, u32[]{:S(2)}) collective-permute-start(bf16[64,1536]{1,0:T(8,128)(2,1)S(1)} %get-tuple-element.240), channel_id=1, source_target_pairs={{0,16},{4,20},{8,24},{12,28},{16,32},{20,36},{24,40},{28,44},{32,4... | collective-permute-start | bytes 589832 | tf_op jit(solution)/shard_map/while/body/eval_jaxpr/ppermute | solution.py:16
  257.1 16.1 %collective-permute-start = (bf16[64,12]{1,0:T(8,128)(2,1)S(1)}, bf16[64,12]{1,0:T(8,128)(2,1)S(1)}, u32[]{:S(2)}, u32[]{:S(2)}) collective-permute-start(bf16[64,12]{1,0:T(8,128)(2,1)S(1)} %get-tuple-element.241), channel_id=1, source_target_pairs={{0,16},{4,20},{8,24},{12,28},{16,32},{20,36},{24,40},{28,44},{32,4... | collective-permute-start | bytes 4616 | tf_op jit(solution)/shard_map/while/body/eval_jaxpr/ppermute | solution.py:16
  274.9 16.2 %collective-permute-start.1 = (bf16[64,1536]{1,0:T(8,128)(2,1)S(1)}, bf16[64,1536]{1,0:T(8,128)(2,1)S(1)}, u32[]{:S(2)}, u32[]{:S(2)}) collective-permute-start(bf16[64,1536]{1,0:T(8,128)(2,1)S(1)} %get-tuple-element.240), channel_id=1, source_target_pairs={{0,16},{4,20},{8,24},{12,28},{16,32},{20,36},{24,40},{28,44},{32,4... | collective-permute-start | bytes 589832 | tf_op jit(solution)/shard_map/while/body/eval_jaxpr/ppermute | solution.py:16
  275.0 16.1 %collective-permute-start = (bf16[64,12]{1,0:T(8,128)(2,1)S(1)}, bf16[64,12]{1,0:T(8,128)(2,1)S(1)}, u32[]{:S(2)}, u32[]{:S(2)}) collective-permute-start(bf16[64,12]{1,0:T(8,128)(2,1)S(1)} %get-tuple-element.241), channel_id=1, source_target_pairs={{0,16},{4,20},{8,24},{12,28},{16,32},{20,36},{24,40},{28,44},{32,4... | collective-permute-start | bytes 4616 | tf_op jit(solution)/shard_map/while/body/eval_jaxpr/ppermute | solution.py:16
  292.9 0.6 copy-start
Sparse Core Ops, SparseCore 0:
  293.7 63.0 all-reduce.1
